TPU v7x, 256 devices: a whole 4x4x8 slice. The times are simulated.
256 devices in a mesh: leaf: 4 (over z_hi), row: 8 (over z_lo, y), col: 8 (over x, core).
Axes of the slice: x: 4, y: 4, z: 8 (z_hi: 4, z_lo: 2; z = z_hi * 2 + z_lo), core: 2. Of those that a mesh axis runs over, the one named last changes fastest.
Arguments:
- lanczos_low: float32 [4, 8, 8, 128, 256], P('leaf', 'col', 'row'), may hold values from -6 to 6
- lanczos_mid: float32 [4, 8, 8, 96, 256], P('leaf', 'col', 'row'), may hold values from -6 to 6
- lanczos_top: float32 [4, 8, 8, 64, 256], P('leaf', 'col', 'row'), may hold values from -6 to 6
- pivot_low: bfloat16 [4, 8192, 8192], P('leaf', 'row', 'col'), as said below
- update_low: bfloat16 [4, 8192, 8192], P('leaf', 'row', 'col'), may hold values from -0.0625 to 0.0625
- pivot_mid: bfloat16 [12288, 24576], P('row', ('leaf', 'col'))
- update_mid: bfloat16 [12288, 16384], P('row', ('leaf', 'col')), may hold values from -0.0546875 to 0.0546875
- pivot_top: bfloat16 [16384, 16384], P('row', ('leaf', 'col'))
- rows_low: int32 [4, 8, 8, 2, 64], P('leaf', 'col', 'row'), may hold values from 0 to 20479, as said below
- rows_mid: int32 [4, 8, 8, 4, 16], P('leaf', 'col', 'row'), may hold values from 0 to 16383, as said below
Outputs:
- solved_low: float32 [4, 8, 8, 128, 256], P('leaf', 'col', 'row')
- solved_mid: float32 [4, 8, 8, 96, 256], P('leaf', 'col', 'row')
- solved_top: float32 [4, 8, 8, 64, 256], P('leaf', 'col', 'row')
Inputs may be any that keep to these rules, and one draw needn't show every extreme that they name: rows_low[2h + a, c, r, s, t] over t are distinct rows of front h, all among pivot rows a 6144 + (c * 8 + r) * 96 + k (0 <= k < 96) and update rows 12288 + a 4096 + (c * 8 + r) * 64 + k (0 <= k < 64); for s = 0 they include the first of those pivot rows and the last of those update rows. rows_mid[q, c, r, 2h + s, t] over s and t are distinct root rows q * 4096 + (c * 8 + r) * 64 + k (0 <= k < 64); for h = 0 they include the first and the last of them. pivot_low, pivot_mid's two square halves and pivot_top are lower triangular.
All inputs are finite; a program needn't handle non-finite values.
Results may differ from a plain program's by a relative error of at most 0.023.
Values may be sent and summed in bfloat16 or wider, within the bound.
No kernel may reach another device: no remote copies, remote signals or barrier semaphores. Data moves between devices by JAX's collectives and lax.ppermute only.
A program may use at most 64 MiB of HBM per device.

v0:
```python
import jax
import jax.numpy as jnp
from jax import lax
from jax.sharding import PartitionSpec as P

P1 = 12288


def from_partner(block, axis, bit):
    count = lax.axis_size(axis)
    route = []
    for low in range(count):
        high = low | 1 << bit
        if high != low and high < count:
            route += [(low, high), (high, low)]
    return lax.ppermute(block, axis, route)


def partner(block_data, leaf_bit):
    return from_partner(block_data.astype(jnp.bfloat16), "leaf", leaf_bit).astype(block_data.dtype)


def forward_apply(matrix, vector, leaf_bits):
    gathered = lax.all_gather(vector, "row", axis=0, tiled=True)
    result = lax.psum_scatter(
        jnp.dot(matrix, gathered, preferred_element_type=jnp.float32),
        "col",
        scatter_dimension=0,
        tiled=True,
    )
    for leaf_bit in leaf_bits:
        result = result + partner(result, leaf_bit)
    return result


def reverse_apply(matrix, vector):
    gathered = lax.all_gather(vector, "col", axis=0, tiled=True)
    return lax.psum_scatter(
        lax.dot_general(
            matrix, gathered, (((0,), (0,)), ((), ())), preferred_element_type=jnp.float32
        ).astype(jnp.bfloat16),
        "row",
        scatter_dimension=0,
        tiled=True,
    ).astype(jnp.float32)


def parent_slot(parent_rows, pivot_local, update_local):
    return jnp.where(
        parent_rows < P1, parent_rows % pivot_local, pivot_local + (parent_rows - P1) % update_local
    )


def pick_span(spans, index_value):
    return lax.dynamic_index_in_dim(spans, index_value, 0, keepdims=False)


def body(
    lanczos_low,
    lanczos_mid,
    lanczos_top,
    pivot_low,
    update_low,
    pivot_mid,
    update_mid,
    pivot_top,
    rows_low,
    rows_mid,
):
    rhs_width = lanczos_low.shape[-1]
    low_in = lanczos_low.reshape(-1, rhs_width)
    mid_in = lanczos_mid.reshape(-1, rhs_width)
    top_in = lanczos_top.reshape(-1, rhs_width)
    pivot_local_low = pivot_low[0]
    update_local_low = update_low[0]
    pivot_local = mid_in.shape[0]
    update_local = update_mid.shape[1] // lax.axis_size("row")
    top_local = top_in.shape[0]
    group_id = lax.axis_index("leaf")
    own_half = group_id % 2
    child_slots = parent_slot(rows_low.reshape(2, -1), pivot_local, update_local)
    root_slots = rows_mid.reshape(4, -1) % top_local
    source_order = jnp.bitwise_xor(group_id, jnp.arange(4, dtype=jnp.int32))
    source_slots = jnp.take(root_slots, source_order, axis=0).reshape(-1)
    own_slots = pick_span(child_slots, own_half)
    other_slots = pick_span(child_slots, 1 - own_half)
    low_y = forward_apply(pivot_local_low, low_in.astype(jnp.bfloat16), ())
    low_c = reverse_apply(update_local_low, low_y.astype(jnp.bfloat16)).reshape(2, -1, rhs_width)
    own_part = pick_span(low_c, own_half)
    came_part = partner(pick_span(low_c, 1 - own_half), 0)
    front_rows = jnp.concatenate([mid_in, jnp.zeros((update_local, rhs_width), mid_in.dtype)], 0)
    front_rows = front_rows.at[own_slots].add(-own_part).at[other_slots].add(-came_part)
    mid_y = forward_apply(pivot_mid, front_rows[:pivot_local].astype(jnp.bfloat16), (0,))
    mid_c = front_rows[pivot_local:] - reverse_apply(update_mid, mid_y.astype(jnp.bfloat16))
    spans = mid_c.reshape(4, -1, rhs_width)
    kept_spans = jnp.stack(
        [pick_span(spans, group_id), pick_span(spans, jnp.bitwise_xor(group_id, 2))]
    )
    moved_spans = partner(
        jnp.stack(
            [
                pick_span(spans, jnp.bitwise_xor(group_id, 1)),
                pick_span(spans, jnp.bitwise_xor(group_id, 3)),
            ]
        ),
        0,
    )
    second = partner(jnp.stack([kept_spans[1], moved_spans[1]]), 1)
    arrived = jnp.stack([kept_spans[0], moved_spans[0], second[0], second[1]]).reshape(
        -1, rhs_width
    )
    top_front = top_in.at[source_slots].add(arrived)
    top_y = forward_apply(pivot_top, top_front.astype(jnp.bfloat16), (0, 1))
    top_x = reverse_apply(pivot_top, top_y.astype(jnp.bfloat16))
    asked_rows = top_x[source_slots].reshape(4, -1, rhs_width)
    back_one = partner(jnp.stack([asked_rows[2], asked_rows[3]]), 1)
    back_zero = partner(jnp.stack([asked_rows[1], back_one[1]]), 0)
    by_root = jnp.stack([asked_rows[0], back_zero[0], back_one[0], back_zero[1]])
    mid_above = jnp.take(by_root, source_order, axis=0).reshape(-1, rhs_width)
    mid_sum = forward_apply(update_mid, mid_above.astype(jnp.bfloat16), (0,))
    mid_x = reverse_apply(pivot_mid, (mid_y - mid_sum).astype(jnp.bfloat16))
    front_values = jnp.concatenate([mid_x, mid_above], 0)
    own_rows = front_values[own_slots]
    got_rows = partner(front_values[other_slots], 0)
    low_above = jnp.where(
        own_half == 0,
        jnp.concatenate([own_rows, got_rows], 0),
        jnp.concatenate([got_rows, own_rows], 0),
    )
    low_sum = forward_apply(update_local_low, low_above.astype(jnp.bfloat16), ())
    low_x = reverse_apply(pivot_local_low, (low_y - low_sum).astype(jnp.bfloat16))
    return (
        low_x.reshape(lanczos_low.shape),
        mid_x.reshape(lanczos_mid.shape),
        top_x.reshape(lanczos_top.shape),
    )


def solution(mesh):
    return jax.shard_map(
        body,
        mesh=mesh,
        in_specs=(
            P("leaf", "col", "row", None, None),
            P("leaf", "col", "row", None, None),
            P("leaf", "col", "row", None, None),
            P("leaf", "row", "col"),
            P("leaf", "row", "col"),
            P("row", ("leaf", "col")),
            P("row", ("leaf", "col")),
            P("row", ("leaf", "col")),
            P("leaf", "col", "row", None, None),
            P("leaf", "col", "row", None, None),
        ),
        out_specs=(
            P("leaf", "col", "row", None, None),
            P("leaf", "col", "row", None, None),
            P("leaf", "col", "row", None, None),
        ),
        check_vma=False,
    )
```

profile of v0, /device:TPU:2, one launch (start us, length us, event | category | flops | bytes accessed | tf_op | source)
XLA Modules:
  0.0 739.1 jit_solution(14551251856389087296)
XLA Ops:
  8.3 29.8 %all-gather = bf16[1,1,1,1024,256]{4,3,2,1,0:T(8,128)(2,1)S(1)} all-gather(bf16[1,1,1,128,256]{4,3,2,1,0:T(8,128)(2,1)S(1)} %convert_element_type.123), channel_id=2, replica_groups=mesh['leaf'=4,'row'=8,'col'=8] {'row'}, dimensions={3}, use_global_device_ids=true | all-gather | bytes 589824 | tf_op jit(solution)/shard_map/all_gather | solution.py:24
  38.1 3.3 fusion.6
  41.5 33.6 %reduce-scatter.25.cloned.1.call-done = f32[128,256]{1,0:T(8,128)} async-done(((f32[1024,256]{1,0:T(8,128)}), f32[128,256]{1,0:T(8,128)}) %reduce-scatter.25.cloned.1.call-update) | async-done | bytes 131088 | tf_op jit(solution)/shard_map/reduce_scatter | solution.py:25
  76.0 13.8 %all_gather.31 = bf16[1024,256]{1,0:T(8,128)(2,1)S(1)} all-gather(bf16[128,256]{1,0:T(8,128)(2,1)S(1)} %convert_element_type.125), channel_id=1, replica_groups=mesh['leaf'=4,'row'=8,'col'=8] {'col'}, dimensions={0}, use_global_device_ids=true | all-gather | bytes 589824 | tf_op jit(solution)/shard_map/all_gather | solution.py:37
  89.8 2.3 fusion.17
  93.3 42.9 %reduce-scatter.31.cloned.1.call-done = bf16[128,256]{1,0:T(8,128)(2,1)} async-done(((bf16[1024,256]{1,0:T(8,128)(2,1)}), bf16[128,256]{1,0:T(8,128)(2,1)}) %reduce-scatter.31.cloned.1.call-update) | async-done | bytes 65552 | tf_op jit(solution)/shard_map/reduce_scatter | solution.py:38
  137.1 2.8 collective-permute-start
  143.3 28.8 %all_gather.32 = bf16[768,256]{1,0:T(8,128)(2,1)S(1)} all-gather(bf16[96,256]{1,0:T(8,128)(2,1)S(1)} %slice.113), channel_id=1, replica_groups=mesh['leaf'=4,'row'=8,'col'=8] {'row'}, dimensions={0}, use_global_device_ids=true | all-gather | bytes 442368 | tf_op jit(solution)/shard_map/all_gather | solution.py:24
  174.1 3.0 copy.45
  177.3 31.0 %reduce-scatter.33.cloned.1.call-done = f32[192,256]{1,0:T(8,128)} async-done(((f32[1536,256]{1,0:T(8,128)}), f32[192,256]{1,0:T(8,128)}) %reduce-scatter.33.cloned.1.call-update) | async-done | bytes 196624
  209.3 2.6 collective-permute-start.1
  212.0 5.8 collective-permute-done.1
  217.9 14.6 %all_gather.33 = bf16[1536,256]{1,0:T(8,128)(2,1)S(1)} all-gather(bf16[192,256]{1,0:T(8,128)(2,1)S(1)} %copy.35), channel_id=1, replica_groups=mesh['leaf'=4,'row'=8,'col'=8] {'col'}, dimensions={0}, use_global_device_ids=true | all-gather | bytes 884736 | tf_op jit(solution)/shard_map/all_gather | solution.py:37
  232.5 2.0 fusion.24
  236.2 41.2 %reduce-scatter.35.cloned.1.call-done = bf16[64,256]{1,0:T(8,128)(2,1)} async-done(((bf16[512,256]{1,0:T(8,128)(2,1)}), bf16[64,256]{1,0:T(8,128)(2,1)}) %reduce-scatter.35.cloned.1.call-update) | async-done | bytes 32784 | tf_op jit(solution)/shard_map/reduce_scatter | solution.py:38
  278.2 2.6 collective-permute-start.2
  280.8 2.2 collective-permute-done.2
  283.0 4.8 collective-permute-start.3
  287.8 2.9 collective-permute-done.3
  291.8 28.4 %all_gather.34 = bf16[512,256]{1,0:T(8,128)(2,1)S(1)} all-gather(bf16[64,256]{1,0:T(8,128)(2,1)S(1)} %convert_element_type.138), channel_id=1, replica_groups=mesh['leaf'=4,'row'=8,'col'=8] {'row'}, dimensions={0}, use_global_device_ids=true | all-gather | bytes 294912 | tf_op jit(solution)/shard_map/all_gather | solution.py:24
  320.1 3.7 convolution_bitcast_fusion.1
  323.9 32.4 %reduce-scatter.27.cloned.1.call-done = f32[256,256]{0,1:T(8,128)} async-done(((f32[2048,256]{0,1:T(8,128)}), f32[256,256]{0,1:T(8,128)}) %reduce-scatter.27.cloned.1.call-update) | async-done | bytes 262160 | tf_op jit(solution)/shard_map/reduce_scatter | solution.py:25
  357.2 2.7 collective-permute-start.4
  359.9 5.9 collective-permute-done.4
  366.8 5.9 collective-permute-start.5
  372.7 6.4 collective-permute-done.5
  380.8 25.4 %all-gather.3.cloned.1.call-done = bf16[2048,256]{0,1:T(8,128)(2,1)} async-done(((bf16[256,256]{0,1:T(8,128)(2,1)}), bf16[2048,256]{0,1:T(8,128)(2,1)}) %all-gather.3.cloned.1.call-update) | async-done | bytes 1048592 | tf_op jit(solution)/shard_map/all_gather | solution.py:37
  406.2 2.6 fusion.25
  409.8 41.9 %reduce-scatter.37.cloned.1.call-done = bf16[64,256]{1,0:T(8,128)(2,1)} async-done(((bf16[512,256]{1,0:T(8,128)(2,1)}), bf16[64,256]{1,0:T(8,128)(2,1)}) %reduce-scatter.37.cloned.1.call-update) | async-done | bytes 32784 | tf_op jit(solution)/shard_map/reduce_scatter | solution.py:38
  453.1 5.1 collective-permute-start.6
  458.3 2.8 collective-permute-done.6
  461.1 2.5 collective-permute-start.7
  463.8 2.0 collective-permute-done.7
  466.4 28.4 %all_gather.36 = bf16[512,256]{1,0:T(8,128)(2,1)S(1)} all-gather(bf16[64,256]{1,0:T(8,128)(2,1)S(1)} %bitcast_select_fusion), channel_id=1, replica_groups=mesh['leaf'=4,'row'=8,'col'=8] {'row'}, dimensions={0}, use_global_device_ids=true | all-gather | bytes 294912 | tf_op jit(solution)/shard_map/all_gather | solution.py:24
  494.8 3.2 convolution_bitcast_fusion
  498.0 3.0 copy.51
  501.1 31.2 %reduce-scatter.39.cloned.1.call-done = f32[192,256]{1,0:T(8,128)} async-done(((f32[1536,256]{1,0:T(8,128)}), f32[192,256]{1,0:T(8,128)}) %reduce-scatter.39.cloned.1.call-update) | async-done | bytes 196624
  533.4 2.6 collective-permute-start.8
  536.0 5.8 collective-permute-done.8
  541.9 14.6 %all_gather.37 = bf16[1536,256]{1,0:T(8,128)(2,1)S(1)} all-gather(bf16[192,256]{1,0:T(8,128)(2,1)S(1)} %copy.38), channel_id=1, replica_groups=mesh['leaf'=4,'row'=8,'col'=8] {'col'}, dimensions={0}, use_global_device_ids=true | all-gather | bytes 884736 | tf_op jit(solution)/shard_map/all_gather | solution.py:37
  558.4 42.1 %reduce-scatter.41.cloned.1.call-done = bf16[96,256]{1,0:T(8,128)(2,1)} async-done(((bf16[768,256]{1,0:T(8,128)(2,1)}), bf16[96,256]{1,0:T(8,128)(2,1)}) %reduce-scatter.41.cloned.1.call-update) | async-done | bytes 49168 | tf_op jit(solution)/shard_map/reduce_scatter | solution.py:38
  601.9 2.6 collective-permute-start.9
  607.1 29.0 %all_gather.38 = bf16[1024,256]{1,0:T(8,128)(2,1)S(1)} all-gather(bf16[128,256]{1,0:T(8,128)(2,1)S(1)} %fusion.29), channel_id=1, replica_groups=mesh['leaf'=4,'row'=8,'col'=8] {'row'}, dimensions={0}, use_global_device_ids=true | all-gather | bytes 589824 | tf_op jit(solution)/shard_map/all_gather | solution.py:24
  636.1 3.3 fusion.8
  639.5 30.3 %reduce-scatter.29.cloned.1.call-done = f32[128,256]{1,0:T(8,128)} async-done(((f32[1024,256]{1,0:T(8,128)}), f32[128,256]{1,0:T(8,128)}) %reduce-scatter.29.cloned.1.call-update) | async-done | bytes 131088 | tf_op jit(solution)/shard_map/reduce_scatter | solution.py:25
  670.6 13.7 %all_gather.39 = bf16[1024,256]{1,0:T(8,128)(2,1)S(1)} all-gather(bf16[128,256]{1,0:T(8,128)(2,1)S(1)} %subtract_convert_fusion.1), channel_id=1, replica_groups=mesh['leaf'=4,'row'=8,'col'=8] {'col'}, dimensions={0}, use_global_device_ids=true | all-gather | bytes 589824 | tf_op jit(solution)/shard_map/all_gather | solution.py:37
  684.4 2.3 fusion.20
  689.0 41.8 %reduce-scatter.43.cloned.1.call-done = bf16[128,256]{1,0:T(8,128)(2,1)} async-done(((bf16[1024,256]{1,0:T(8,128)(2,1)}), bf16[128,256]{1,0:T(8,128)(2,1)}) %reduce-scatter.43.cloned.1.call-update) | async-done | bytes 65552
  (110 shorter events, 33.2 us)
Async XLA Ops:
  7.2 165.0 %copy-start = (bf16[1536,768]{1,0:T(8,128)(2,1)S(1)}, bf16[1536,768]{1,0:T(8,128)(2,1)}, u32[]{:S(2)}) copy-start(bf16[1536,768]{1,0:T(8,128)(2,1)} %param.15) | copy-start | bytes 7077892
  7.2 67.9 %reduce-scatter.25.cloned.1.call-start = ((), (), s32[]{:S(2)}) async-start(), calls=%async_computation.10 | async-start | bytes 1179648 | tf_op jit(solution)/shard_map/reduce_scatter | solution.py:25
  41.4 94.8 %reduce-scatter.31.cloned.1.call-start = ((), (), s32[]{:S(2)}) async-start(), calls=%async_computation.14 | async-start | bytes 589824 | tf_op jit(solution)/shard_map/reduce_scatter | solution.py:38
  89.8 3.5 copy-start.7
  89.8 50.1 %copy-start.5 = (f32[1,1,1,96,256]{4,3,2,1,0:T(8,128)S(1)}, f32[1,1,1,96,256]{4,3,2,1,0:T(8,128)}, u32[]{:S(2)}) copy-start(f32[1,1,1,96,256]{4,3,2,1,0:T(8,128)} %param.11) | copy-start | bytes 294916
  93.2 115.1 %reduce-scatter.33.cloned.1.call-start = ((), (), s32[]{:S(2)}) async-start(), calls=%async_computation.15 | async-start | bytes 1769472
  137.1 5.2 collective-permute-start
  177.2 100.2 %reduce-scatter.35.cloned.1.call-start = ((), (), s32[]{:S(2)}) async-start(), calls=%async_computation.16 | async-start | bytes 294912 | tf_op jit(solution)/shard_map/reduce_scatter | solution.py:38
  209.3 8.4 %collective-permute-start.1 = (bf16[192,256]{0,1:T(8,128)(2,1)S(1)}, bf16[192,256]{0,1:T(8,128)(2,1)S(1)}, u32[]{:S(2)}, u32[]{:S(2)}) collective-permute-start(bf16[192,256]{0,1:T(8,128)(2,1)S(1)} %convert_element_type.131), channel_id=1, source_target_pairs={{0,64},{64,0},{128,192},{192,128},{1,65},{65,1},{129,193},{193,129... | collective-permute-start | bytes 294920 | tf_op jit(solution)/shard_map/ppermute | solution.py:16
  217.9 17.6 %copy-start.6 = (s32[1,1,1,4,16]{4,3,2,1,0:T(4,128)S(1)}, s32[1,1,1,4,16]{4,3,2,1,0:T(4,128)}, u32[]{:S(2)}) copy-start(s32[1,1,1,4,16]{4,3,2,1,0:T(4,128)} %param.19) | copy-start | bytes 772
  232.5 58.2 %copy-start.1 = (f32[1,1,1,64,256]{4,3,2,1,0:T(8,128)S(1)}, f32[1,1,1,64,256]{4,3,2,1,0:T(8,128)}, u32[]{:S(2)}) copy-start(f32[1,1,1,64,256]{4,3,2,1,0:T(8,128)} %param.12) | copy-start | bytes 196612
  235.4 120.9 %reduce-scatter.27.cloned.1.call-start = ((), (), s32[]{:S(2)}) async-start(), calls=%async_computation.11 | async-start | bytes 2359296 | tf_op jit(solution)/shard_map/reduce_scatter | solution.py:25
  278.2 4.8 collective-permute-start.2
  283.0 7.7 %collective-permute-start.3 = (bf16[2,16,256]{2,1,0:T(8,128)(2,1)S(1)}, bf16[2,16,256]{2,1,0:T(8,128)(2,1)S(1)}, u32[]{:S(2)}, u32[]{:S(2)}) collective-permute-start(bf16[2,16,256]{2,1,0:T(8,128)(2,1)S(1)} %pad_maximum_fusion.4), channel_id=1, source_target_pairs={{0,128},{128,0},{64,192},{192,64},{1,129},{129,1},{65,193},{193,65... | collective-permute-start | bytes 49160 | tf_op jit(solution)/shard_map/ppermute | solution.py:16
  323.9 82.4 %all-gather.3.cloned.1.call-start = ((), (), s32[]{:S(2)}) async-start(), calls=%async_computation.12 | async-start | bytes 1179648 | tf_op jit(solution)/shard_map/all_gather | solution.py:37
  357.2 8.6 %collective-permute-start.4 = (bf16[256,256]{0,1:T(8,128)(2,1)S(1)}, bf16[256,256]{0,1:T(8,128)(2,1)S(1)}, u32[]{:S(2)}, u32[]{:S(2)}) collective-permute-start(bf16[256,256]{0,1:T(8,128)(2,1)S(1)} %convert_element_type.139), channel_id=1, source_target_pairs={{0,64},{64,0},{128,192},{192,128},{1,65},{65,1},{129,193},{193,129... | collective-permute-start | bytes 393224 | tf_op jit(solution)/shard_map/ppermute | solution.py:16
  366.8 12.3 %collective-permute-start.5 = (bf16[256,256]{0,1:T(8,128)(2,1)S(1)}, bf16[256,256]{0,1:T(8,128)(2,1)S(1)}, u32[]{:S(2)}, u32[]{:S(2)}) collective-permute-start(bf16[256,256]{0,1:T(8,128)(2,1)S(1)} %fusion.28), channel_id=1, source_target_pairs={{0,128},{128,0},{64,192},{192,64},{1,129},{129,1},{65,193},{193,65... | collective-permute-start | bytes 393224 | tf_op jit(solution)/shard_map/ppermute | solution.py:16
  380.7 71.0 %reduce-scatter.37.cloned.1.call-start = ((), (), s32[]{:S(2)}) async-start(), calls=%async_computation.17 | async-start | bytes 294912 | tf_op jit(solution)/shard_map/reduce_scatter | solution.py:38
  409.7 122.6 %reduce-scatter.39.cloned.1.call-start = ((), (), s32[]{:S(2)}) async-start(), calls=%async_computation.18 | async-start | bytes 1769472
  453.1 7.9 %collective-permute-start.6 = (bf16[2,16,256]{2,1,0:T(8,128)(2,1)S(1)}, bf16[2,16,256]{2,1,0:T(8,128)(2,1)S(1)}, u32[]{:S(2)}, u32[]{:S(2)}) collective-permute-start(bf16[2,16,256]{2,1,0:T(8,128)(2,1)S(1)} %pad_maximum_fusion.5), channel_id=1, source_target_pairs={{0,128},{128,0},{64,192},{192,64},{1,129},{129,1},{65,193},{193,65... | collective-permute-start | bytes 49160 | tf_op jit(solution)/shard_map/ppermute | solution.py:16
  461.1 4.7 collective-permute-start.7
  501.1 99.4 %reduce-scatter.41.cloned.1.call-start = ((), (), s32[]{:S(2)}) async-start(), calls=%async_computation.19 | async-start | bytes 442368 | tf_op jit(solution)/shard_map/reduce_scatter | solution.py:38
  533.4 8.4 %collective-permute-start.8 = (bf16[192,256]{0,1:T(8,128)(2,1)S(1)}, bf16[192,256]{0,1:T(8,128)(2,1)S(1)}, u32[]{:S(2)}, u32[]{:S(2)}) collective-permute-start(bf16[192,256]{0,1:T(8,128)(2,1)S(1)} %convert_element_type.149), channel_id=1, source_target_pairs={{0,64},{64,0},{128,192},{192,128},{1,65},{65,1},{129,193},{193,129... | collective-permute-start | bytes 294920 | tf_op jit(solution)/shard_map/ppermute | solution.py:16
  558.3 111.4 %reduce-scatter.29.cloned.1.call-start = ((), (), s32[]{:S(2)}) async-start(), calls=%async_computation.13 | async-start | bytes 1179648 | tf_op jit(solution)/shard_map/reduce_scatter | solution.py:25
  601.9 5.1 collective-permute-start.9
  636.1 33.7 %copy-start.3 = (f32[128,256]{1,0:T(8,128)S(1)}, f32[128,256]{1,0:T(8,128)}, u32[]{:S(2)}) copy-start(f32[128,256]{1,0:T(8,128)} %reduce-scatter.25.cloned.1.call-done) | copy-start | bytes 393220
  639.4 91.4 %reduce-scatter.43.cloned.1.call-start = ((), (), s32[]{:S(2)}) async-start(), calls=%async_computation.20 | async-start | bytes 589824
  684.4 3.4 copy-start.2
  684.4 4.0 copy-start.4
Sparse Core Ops, SparseCore 0:
  41.6 33.4 reduce-scatter.24
  93.3 42.8 reduce-scatter.30
  177.3 30.8 reduce-scatter.32
  235.5 41.8 reduce-scatter.34
  324.0 32.2 reduce-scatter.26
  380.9 25.3 all-gather.2
  409.8 41.8 reduce-scatter.36
  501.2 31.0 reduce-scatter.38
  558.4 41.9 reduce-scatter.40
  639.5 30.1 reduce-scatter.28
  687.9 42.9 reduce-scatter.42
where the time goes:
time: 740 us; the launch traced here: 739 us
  waiting for transfers between devices  431 us (58%)
  blocking collectives  201 us (27%)
  starting transfers between devices  34.8 us (5%)
  matrix products  25.6 us (3%)
  local copies, waits for them, and re-layouts  19 us (3%)
  between operations  14.2 us (2%)
  other arithmetic  13.7 us (2%)
    reduce_scatter x4, waiting for transfers between devices, reverse_apply(): lax.psum_scatter(lax.dot_general(matrix, gathered, (((0,), (0,)), ((), ()...  168 us
    all_gather x5, blocking collectives, forward_apply(): gathered = lax.all_gather(vector, 'row', axis=0, tiled=True)  144 us
    unnamed x14, waiting for transfers between devices  104 us
    reduce_scatter x3, waiting for transfers between devices, forward_apply(): lax.psum_scatter(jnp.dot(matrix, gathered, preferred_element_type=jnp.flo...  96.2 us
    all_gather x4, blocking collectives, reverse_apply(): gathered = lax.all_gather(vector, 'col', axis=0, tiled=True)  56.7 us
    ppermute x10, waiting for transfers between devices, from_partner(): return lax.ppermute(block, axis, route)  36.8 us
    ppermute x10, starting transfers between devices, from_partner(): return lax.ppermute(block, axis, route)  34.3 us
    all_gather x1, waiting for transfers between devices, reverse_apply(): gathered = lax.all_gather(vector, 'col', axis=0, tiled=True)  25.4 us
  transfers between devices with their start and end apart: 21, of which 21 were waited for; matrix products, arithmetic and copies ran while one was open for 1% of the time, Pallas kernels for 0%

commit v1 on v0

--- a/solution.py
+++ b/solution.py
@@ -1,9 +1,20 @@
+import functools
 import jax
 import jax.numpy as jnp
 from jax import lax
 from jax.sharding import PartitionSpec as P
 
 P1 = 12288
+
+
+def save_records_on_mesh(frame, mesh_ax):
+    odd = jnp.stack([frame for _ in range(lax.axis_size(mesh_ax))])
+    carry_in = lax.all_to_all(odd, mesh_ax, 0, 0)
+    mixed_arr = jnp.concatenate(carry_in, axis=0)
+    return mixed_arr
+
+
+core_do = functools.partial(save_records_on_mesh, mesh_ax="row")
 
 
 def from_partner(block, axis, bit):
@@ -21,7 +32,7 @@
 
 
 def forward_apply(matrix, vector, leaf_bits):
-    gathered = lax.all_gather(vector, "row", axis=0, tiled=True)
+    gathered = core_do(vector)
     result = lax.psum_scatter(
         jnp.dot(matrix, gathered, preferred_element_type=jnp.float32),
         "col",

time: 740 us -> 650 us (0.88)
  blocking collectives: 201 us -> 113 us
    all_gather x5 -> x0, blocking collectives: 144 us -> none  [forward_apply(): gathered = lax.all_gather(vector, 'row', axis=0, tiled=True)]
    all_to_all x0 -> x5, blocking collectives: none -> 56.7 us  [save_records_on_mesh(): carry_in = lax.all_to_all(odd, mesh_ax, 0, 0)]
where the time goes in v1:
time: 650 us; the launch traced here: 649 us
  waiting for transfers between devices  428 us (66%)
  blocking collectives  113 us (17%)
  starting transfers between devices  34.8 us (5%)
  matrix products  25.6 us (4%)
  local copies, waits for them, and re-layouts  19.1 us (3%)
  between operations  14.3 us (2%)
  other arithmetic  13.7 us (2%)
    reduce_scatter x4, waiting for transfers between devices, reverse_apply(): lax.psum_scatter(lax.dot_general(matrix, gathered, (((0,), (0,)), ((), ()...  168 us
    unnamed x14, waiting for transfers between devices  104 us
    reduce_scatter x3, waiting for transfers between devices, forward_apply(): lax.psum_scatter(jnp.dot(matrix, gathered, preferred_element_type=jnp.flo...  93.4 us
    all_gather x4, blocking collectives, reverse_apply(): gathered = lax.all_gather(vector, 'col', axis=0, tiled=True)  56.8 us
    all_to_all x5, blocking collectives, save_records_on_mesh(): carry_in = lax.all_to_all(odd, mesh_ax, 0, 0)  56.7 us
    ppermute x10, waiting for transfers between devices, from_partner(): return lax.ppermute(block, axis, route)  36.9 us
    ppermute x10, starting transfers between devices, from_partner(): return lax.ppermute(block, axis, route)  34.4 us
    all_gather x1, waiting for transfers between devices, reverse_apply(): gathered = lax.all_gather(vector, 'col', axis=0, tiled=True)  25.4 us
  transfers between devices with their start and end apart: 21, of which 21 were waited for; matrix products, arithmetic and copies ran while one was open for 1% of the time, Pallas kernels for 0%

profile of v1, /device:TPU:2, one launch (start us, length us, event | category | flops | bytes accessed | tf_op | source)
XLA Modules:
  0.0 648.8 jit_solution(7357442035881450778)
XLA Ops:
  8.3 15.7 %all_to_all.25 = bf16[8,128,256]{2,1,0:T(8,128)(2,1)S(1)} all-to-all(bf16[8,128,256]{2,1,0:T(8,128)(2,1)S(1)} %stack.27), channel_id=1, replica_groups=mesh['leaf'=4,'row'=8,'col'=8] {'row'}, dimensions={0} | all-to-all | bytes 1048576 | tf_op jit(solution)/shard_map/all_to_all | solution.py:12
  24.0 3.3 fusion.6
  27.4 31.6 %reduce-scatter.25.cloned.1.call-done = f32[128,256]{1,0:T(8,128)} async-done(((f32[1024,256]{1,0:T(8,128)}), f32[128,256]{1,0:T(8,128)}) %reduce-scatter.25.cloned.1.call-update) | async-done | bytes 131088 | tf_op jit(solution)/shard_map/reduce_scatter | solution.py:36
  59.9 13.8 %all_gather.15 = bf16[1024,256]{1,0:T(8,128)(2,1)S(1)} all-gather(bf16[128,256]{1,0:T(8,128)(2,1)S(1)} %convert_element_type.131), channel_id=1, replica_groups=mesh['leaf'=4,'row'=8,'col'=8] {'col'}, dimensions={0}, use_global_device_ids=true | all-gather | bytes 589824 | tf_op jit(solution)/shard_map/all_gather | solution.py:48
  73.7 2.4 fusion.17
  77.2 43.0 %reduce-scatter.31.cloned.1.call-done = bf16[128,256]{1,0:T(8,128)(2,1)} async-done(((bf16[1024,256]{1,0:T(8,128)(2,1)}), bf16[128,256]{1,0:T(8,128)(2,1)}) %reduce-scatter.31.cloned.1.call-update) | async-done | bytes 65552 | tf_op jit(solution)/shard_map/reduce_scatter | solution.py:49
  121.1 2.7 collective-permute-start
  127.4 10.4 %all_to_all.26 = bf16[8,96,256]{2,1,0:T(8,128)(2,1)S(1)} all-to-all(bf16[8,96,256]{2,1,0:T(8,128)(2,1)S(1)} %stack.28), channel_id=1, replica_groups=mesh['leaf'=4,'row'=8,'col'=8] {'row'}, dimensions={0} | all-to-all | bytes 786432 | tf_op jit(solution)/shard_map/all_to_all | solution.py:12
  139.7 3.0 copy.48
  142.9 31.0 %reduce-scatter.33.cloned.1.call-done = f32[192,256]{1,0:T(8,128)} async-done(((f32[1536,256]{1,0:T(8,128)}), f32[192,256]{1,0:T(8,128)}) %reduce-scatter.33.cloned.1.call-update) | async-done | bytes 196624
  175.0 2.7 collective-permute-start.1
  177.6 5.7 collective-permute-done.1
  183.5 14.6 %all_gather.16 = bf16[1536,256]{1,0:T(8,128)(2,1)S(1)} all-gather(bf16[192,256]{1,0:T(8,128)(2,1)S(1)} %copy.38), channel_id=1, replica_groups=mesh['leaf'=4,'row'=8,'col'=8] {'col'}, dimensions={0}, use_global_device_ids=true | all-gather | bytes 884736 | tf_op jit(solution)/shard_map/all_gather | solution.py:48
  198.1 2.0 fusion.24
  201.8 41.1 %reduce-scatter.35.cloned.1.call-done = bf16[64,256]{1,0:T(8,128)(2,1)} async-done(((bf16[512,256]{1,0:T(8,128)(2,1)}), bf16[64,256]{1,0:T(8,128)(2,1)}) %reduce-scatter.35.cloned.1.call-update) | async-done | bytes 32784 | tf_op jit(solution)/shard_map/reduce_scatter | solution.py:49
  243.7 2.6 collective-permute-start.2
  246.3 2.2 collective-permute-done.2
  248.5 4.9 collective-permute-start.3
  253.4 2.9 collective-permute-done.3
  257.3 9.9 %all_to_all.27 = bf16[8,64,256]{2,1,0:T(8,128)(2,1)S(1)} all-to-all(bf16[8,64,256]{2,1,0:T(8,128)(2,1)S(1)} %stack.32), channel_id=1, replica_groups=mesh['leaf'=4,'row'=8,'col'=8] {'row'}, dimensions={0} | all-to-all | bytes 524288 | tf_op jit(solution)/shard_map/all_to_all | solution.py:12
  267.2 3.7 convolution_bitcast_fusion.1
  271.0 31.6 %reduce-scatter.27.cloned.1.call-done = f32[256,256]{0,1:T(8,128)} async-done(((f32[2048,256]{0,1:T(8,128)}), f32[256,256]{0,1:T(8,128)}) %reduce-scatter.27.cloned.1.call-update) | async-done | bytes 262160 | tf_op jit(solution)/shard_map/reduce_scatter | solution.py:36
  303.5 2.6 collective-permute-start.4
  306.2 5.9 collective-permute-done.4
  313.1 5.9 collective-permute-start.5
  319.0 6.4 collective-permute-done.5
  327.1 25.4 %all-gather.2.cloned.1.call-done = bf16[2048,256]{0,1:T(8,128)(2,1)} async-done(((bf16[256,256]{0,1:T(8,128)(2,1)}), bf16[2048,256]{0,1:T(8,128)(2,1)}) %all-gather.2.cloned.1.call-update) | async-done | bytes 1048592 | tf_op jit(solution)/shard_map/all_gather | solution.py:48
  352.5 2.6 fusion.25
  356.0 41.9 %reduce-scatter.37.cloned.1.call-done = bf16[64,256]{1,0:T(8,128)(2,1)} async-done(((bf16[512,256]{1,0:T(8,128)(2,1)}), bf16[64,256]{1,0:T(8,128)(2,1)}) %reduce-scatter.37.cloned.1.call-update) | async-done | bytes 32784 | tf_op jit(solution)/shard_map/reduce_scatter | solution.py:49
  399.4 5.1 collective-permute-start.6
  404.6 2.8 collective-permute-done.6
  407.3 2.5 collective-permute-start.7
  410.0 2.0 collective-permute-done.7
  412.7 9.7 %all_to_all.28 = bf16[8,64,256]{2,1,0:T(8,128)(2,1)S(1)} all-to-all(bf16[8,64,256]{2,1,0:T(8,128)(2,1)S(1)} %stack.36), channel_id=1, replica_groups=mesh['leaf'=4,'row'=8,'col'=8] {'row'}, dimensions={0} | all-to-all | bytes 524288 | tf_op jit(solution)/shard_map/all_to_all | solution.py:12
  422.4 3.2 convolution_bitcast_fusion
  425.6 3.0 copy.54
  428.7 31.0 %reduce-scatter.39.cloned.1.call-done = f32[192,256]{1,0:T(8,128)} async-done(((f32[1536,256]{1,0:T(8,128)}), f32[192,256]{1,0:T(8,128)}) %reduce-scatter.39.cloned.1.call-update) | async-done | bytes 196624
  460.8 2.6 collective-permute-start.8
  463.4 5.7 collective-permute-done.8
  469.3 14.6 %all_gather.18 = bf16[1536,256]{1,0:T(8,128)(2,1)S(1)} all-gather(bf16[192,256]{1,0:T(8,128)(2,1)S(1)} %copy.41), channel_id=1, replica_groups=mesh['leaf'=4,'row'=8,'col'=8] {'col'}, dimensions={0}, use_global_device_ids=true | all-gather | bytes 884736 | tf_op jit(solution)/shard_map/all_gather | solution.py:48
  485.7 42.2 %reduce-scatter.41.cloned.1.call-done = bf16[96,256]{1,0:T(8,128)(2,1)} async-done(((bf16[768,256]{1,0:T(8,128)(2,1)}), bf16[96,256]{1,0:T(8,128)(2,1)}) %reduce-scatter.41.cloned.1.call-update) | async-done | bytes 49168 | tf_op jit(solution)/shard_map/reduce_scatter | solution.py:49
  529.5 2.7 collective-permute-start.9
  534.8 11.0 %all_to_all.29 = bf16[8,128,256]{2,1,0:T(8,128)(2,1)S(1)} all-to-all(bf16[8,128,256]{2,1,0:T(8,128)(2,1)S(1)} %stack.37), channel_id=1, replica_groups=mesh['leaf'=4,'row'=8,'col'=8] {'row'}, dimensions={0} | all-to-all | bytes 1048576 | tf_op jit(solution)/shard_map/all_to_all | solution.py:12
  545.8 3.3 fusion.8
  549.2 30.2 %reduce-scatter.29.cloned.1.call-done = f32[128,256]{1,0:T(8,128)} async-done(((f32[1024,256]{1,0:T(8,128)}), f32[128,256]{1,0:T(8,128)}) %reduce-scatter.29.cloned.1.call-update) | async-done | bytes 131088 | tf_op jit(solution)/shard_map/reduce_scatter | solution.py:36
  580.3 13.8 %all_gather.19 = bf16[1024,256]{1,0:T(8,128)(2,1)S(1)} all-gather(bf16[128,256]{1,0:T(8,128)(2,1)S(1)} %subtract_convert_fusion.1), channel_id=1, replica_groups=mesh['leaf'=4,'row'=8,'col'=8] {'col'}, dimensions={0}, use_global_device_ids=true | all-gather | bytes 589824 | tf_op jit(solution)/shard_map/all_gather | solution.py:48
  594.1 2.3 fusion.20
  598.8 41.8 %reduce-scatter.43.cloned.1.call-done = bf16[128,256]{1,0:T(8,128)(2,1)} async-done(((bf16[1024,256]{1,0:T(8,128)(2,1)}), bf16[128,256]{1,0:T(8,128)(2,1)}) %reduce-scatter.43.cloned.1.call-update) | async-done | bytes 65552
  (115 shorter events, 33.4 us)
Async XLA Ops:
  7.2 130.6 %copy-start = (bf16[1536,768]{1,0:T(8,128)(2,1)S(1)}, bf16[1536,768]{1,0:T(8,128)(2,1)}, u32[]{:S(2)}) copy-start(bf16[1536,768]{1,0:T(8,128)(2,1)} %param.15) | copy-start | bytes 7077892
  7.2 51.8 %reduce-scatter.25.cloned.1.call-start = ((), (), s32[]{:S(2)}) async-start(), calls=%async_computation.15 | async-start | bytes 1179648 | tf_op jit(solution)/shard_map/reduce_scatter | solution.py:36
  27.3 92.9 %reduce-scatter.31.cloned.1.call-start = ((), (), s32[]{:S(2)}) async-start(), calls=%async_computation.19 | async-start | bytes 589824 | tf_op jit(solution)/shard_map/reduce_scatter | solution.py:49
  73.7 3.5 copy-start.7
  73.7 50.1 %copy-start.5 = (f32[1,1,1,96,256]{4,3,2,1,0:T(8,128)S(1)}, f32[1,1,1,96,256]{4,3,2,1,0:T(8,128)}, u32[]{:S(2)}) copy-start(f32[1,1,1,96,256]{4,3,2,1,0:T(8,128)} %param.11) | copy-start | bytes 294916
  77.1 96.8 %reduce-scatter.33.cloned.1.call-start = ((), (), s32[]{:S(2)}) async-start(), calls=%async_computation.20 | async-start | bytes 1769472
  121.1 5.2 collective-permute-start
  142.8 100.2 %reduce-scatter.35.cloned.1.call-start = ((), (), s32[]{:S(2)}) async-start(), calls=%async_computation.21 | async-start | bytes 294912 | tf_op jit(solution)/shard_map/reduce_scatter | solution.py:49
  175.0 8.4 %collective-permute-start.1 = (bf16[192,256]{0,1:T(8,128)(2,1)S(1)}, bf16[192,256]{0,1:T(8,128)(2,1)S(1)}, u32[]{:S(2)}, u32[]{:S(2)}) collective-permute-start(bf16[192,256]{0,1:T(8,128)(2,1)S(1)} %convert_element_type.137), channel_id=1, source_target_pairs={{0,64},{64,0},{128,192},{192,128},{1,65},{65,1},{129,193},{193,129... | collective-permute-start | bytes 294920 | tf_op jit(solution)/shard_map/ppermute | solution.py:27
  183.5 17.6 %copy-start.6 = (s32[1,1,1,4,16]{4,3,2,1,0:T(4,128)S(1)}, s32[1,1,1,4,16]{4,3,2,1,0:T(4,128)}, u32[]{:S(2)}) copy-start(s32[1,1,1,4,16]{4,3,2,1,0:T(4,128)} %param.19) | copy-start | bytes 772
  198.1 58.1 %copy-start.1 = (f32[1,1,1,64,256]{4,3,2,1,0:T(8,128)S(1)}, f32[1,1,1,64,256]{4,3,2,1,0:T(8,128)}, u32[]{:S(2)}) copy-start(f32[1,1,1,64,256]{4,3,2,1,0:T(8,128)} %param.12) | copy-start | bytes 196612
  201.0 101.5 %reduce-scatter.27.cloned.1.call-start = ((), (), s32[]{:S(2)}) async-start(), calls=%async_computation.16 | async-start | bytes 2359296 | tf_op jit(solution)/shard_map/reduce_scatter | solution.py:36
  243.7 4.8 collective-permute-start.2
  248.5 7.7 %collective-permute-start.3 = (bf16[2,16,256]{2,1,0:T(8,128)(2,1)S(1)}, bf16[2,16,256]{2,1,0:T(8,128)(2,1)S(1)}, u32[]{:S(2)}, u32[]{:S(2)}) collective-permute-start(bf16[2,16,256]{2,1,0:T(8,128)(2,1)S(1)} %pad_maximum_fusion.4), channel_id=1, source_target_pairs={{0,128},{128,0},{64,192},{192,64},{1,129},{129,1},{65,193},{193,65... | collective-permute-start | bytes 49160 | tf_op jit(solution)/shard_map/ppermute | solution.py:27
  270.9 81.6 %all-gather.2.cloned.1.call-start = ((), (), s32[]{:S(2)}) async-start(), calls=%async_computation.17 | async-start | bytes 1179648 | tf_op jit(solution)/shard_map/all_gather | solution.py:48
  303.5 8.6 %collective-permute-start.4 = (bf16[256,256]{0,1:T(8,128)(2,1)S(1)}, bf16[256,256]{0,1:T(8,128)(2,1)S(1)}, u32[]{:S(2)}, u32[]{:S(2)}) collective-permute-start(bf16[256,256]{0,1:T(8,128)(2,1)S(1)} %convert_element_type.145), channel_id=1, source_target_pairs={{0,64},{64,0},{128,192},{192,128},{1,65},{65,1},{129,193},{193,129... | collective-permute-start | bytes 393224 | tf_op jit(solution)/shard_map/ppermute | solution.py:27
  313.1 12.3 %collective-permute-start.5 = (bf16[256,256]{0,1:T(8,128)(2,1)S(1)}, bf16[256,256]{0,1:T(8,128)(2,1)S(1)}, u32[]{:S(2)}, u32[]{:S(2)}) collective-permute-start(bf16[256,256]{0,1:T(8,128)(2,1)S(1)} %fusion.27), channel_id=1, source_target_pairs={{0,128},{128,0},{64,192},{192,64},{1,129},{129,1},{65,193},{193,65... | collective-permute-start | bytes 393224 | tf_op jit(solution)/shard_map/ppermute | solution.py:27
  327.1 70.9 %reduce-scatter.37.cloned.1.call-start = ((), (), s32[]{:S(2)}) async-start(), calls=%async_computation.22 | async-start | bytes 294912 | tf_op jit(solution)/shard_map/reduce_scatter | solution.py:49
  356.0 103.7 %reduce-scatter.39.cloned.1.call-start = ((), (), s32[]{:S(2)}) async-start(), calls=%async_computation.23 | async-start | bytes 1769472
  399.4 7.9 %collective-permute-start.6 = (bf16[2,16,256]{2,1,0:T(8,128)(2,1)S(1)}, bf16[2,16,256]{2,1,0:T(8,128)(2,1)S(1)}, u32[]{:S(2)}, u32[]{:S(2)}) collective-permute-start(bf16[2,16,256]{2,1,0:T(8,128)(2,1)S(1)} %pad_maximum_fusion.5), channel_id=1, source_target_pairs={{0,128},{128,0},{64,192},{192,64},{1,129},{129,1},{65,193},{193,65... | collective-permute-start | bytes 49160 | tf_op jit(solution)/shard_map/ppermute | solution.py:27
  407.3 4.7 collective-permute-start.7
  428.7 99.3 %reduce-scatter.41.cloned.1.call-start = ((), (), s32[]{:S(2)}) async-start(), calls=%async_computation.24 | async-start | bytes 442368 | tf_op jit(solution)/shard_map/reduce_scatter | solution.py:49
  460.8 8.4 %collective-permute-start.8 = (bf16[192,256]{0,1:T(8,128)(2,1)S(1)}, bf16[192,256]{0,1:T(8,128)(2,1)S(1)}, u32[]{:S(2)}, u32[]{:S(2)}) collective-permute-start(bf16[192,256]{0,1:T(8,128)(2,1)S(1)} %convert_element_type.155), channel_id=1, source_target_pairs={{0,64},{64,0},{128,192},{192,128},{1,65},{65,1},{129,193},{193,129... | collective-permute-start | bytes 294920 | tf_op jit(solution)/shard_map/ppermute | solution.py:27
  485.7 93.7 %reduce-scatter.29.cloned.1.call-start = ((), (), s32[]{:S(2)}) async-start(), calls=%async_computation.18 | async-start | bytes 1179648 | tf_op jit(solution)/shard_map/reduce_scatter | solution.py:36
  529.5 5.3 collective-permute-start.9
  545.8 33.6 %copy-start.3 = (f32[128,256]{1,0:T(8,128)S(1)}, f32[128,256]{1,0:T(8,128)}, u32[]{:S(2)}) copy-start(f32[128,256]{1,0:T(8,128)} %reduce-scatter.25.cloned.1.call-done) | copy-start | bytes 393220
  549.2 91.4 %reduce-scatter.43.cloned.1.call-start = ((), (), s32[]{:S(2)}) async-start(), calls=%async_computation.25 | async-start | bytes 589824
  594.1 3.4 copy-start.2
  594.1 4.0 copy-start.4
Sparse Core Ops, SparseCore 0:
  27.5 31.5 reduce-scatter.24
  77.2 42.9 reduce-scatter.30
  142.9 30.9 reduce-scatter.32
  201.1 41.7 reduce-scatter.34
  271.0 31.4 reduce-scatter.26
  327.2 25.2 all-gather.1
  356.1 41.8 reduce-scatter.36
  428.8 30.8 reduce-scatter.38
  485.8 42.1 reduce-scatter.40
  549.3 30.0 reduce-scatter.28
  597.6 42.9 reduce-scatter.42
